TPU v7x, 512 devices: a whole 4x4x16 slice. The times are simulated.
512 devices in a mesh: row: 16 (over x, y), col: 32 (over z, core).
Axes of the slice: x: 4, y: 4, z: 16, core: 2. Of those that a mesh axis runs over, the one named last changes fastest.
Arguments:
- observed: int32 [32, 3072, 2048], P('col', 'row'), may hold values from 0 to 1, as said below
- user_effect: float32 [32, 3072], P('col', 'row'), may hold values from -4 to 4
- item_effect: float32 [128, 128], replicated, may hold values from -4 to 4
- block_list: int32 [32, 16], replicated, may hold values from 0 to 127, as said below
Outputs:
- factored: float32 [8, 16, 128, 4, 32, 128], P(None, 'row', None, None, 'col')
- correction: bfloat16 [8, 16, 128, 4, 32, 128], P(None, 'row', None, None, 'col')
- logdet: float32 [], replicated
- pivots: float32 [16, 32, 32], P('row', 'col')
Inputs may be any that keep to these rules, and one draw needn't show every extreme that they name: `block_list`: each row lists 16 distinct tiles; entry k has remainder k // (16 // 16) modulo 16; at most max(1, 16 // 32) entries of a row share a remainder modulo 32, and some remainder reaches that count in every row. `observed`: 1 marks a rating of the user for the item.
All inputs are finite; a program needn't handle non-finite values.
Results may differ from a plain program's by a relative error of at most 0.0069.
Values may be sent and summed in bfloat16 or wider, within the bound.
No kernel may reach another device: no remote copies, remote signals or barrier semaphores. Data moves between devices by JAX's collectives and lax.ppermute only.
A program may use at most 128 MiB of HBM per device.

v0:
```python
import jax
import jax.numpy as jnp
from jax import lax
from jax.sharding import PartitionSpec as P

PANEL_BLOCKS = 2


highest = lax.Precision.HIGHEST
user_prior = 1.0
item_prior = 1.0


def broadcast(block, axis, source):
    block = jnp.where(lax.axis_index(axis) == source, block, jnp.zeros_like(block))
    return lax.psum(block, axis)


def body(observed, user_effect, item_effect, block_list):
    rows_n = lax.axis_size("row")
    cols_n = lax.axis_size("col")
    row_idx = lax.axis_index("row")
    col_idx = lax.axis_index("col")
    nblocks, tile = item_effect.shape
    kcount = block_list.shape[1]
    per_row = kcount // rows_n
    slots = max(1, kcount // cols_n)
    width = kcount * tile
    group = per_row * tile
    nb_r = nblocks // rows_n
    nb_c = nblocks // cols_n
    mine = lax.dynamic_index_in_dim(block_list, col_idx, 0, keepdims=False)
    picker = (mine[:, None] == jnp.arange(nblocks)[None, :]).astype(jnp.float32)
    item_vals = jnp.dot(picker, item_effect, precision=highest).reshape(width)
    marks = observed[0]
    prob = jax.nn.sigmoid(user_effect[0][:, None] + item_vals[None, :])
    weight = jnp.where(marks > 0, prob * (1.0 - prob), 0.0)
    precision_u = user_prior + jnp.sum(weight, axis=1)
    scaled = (weight / jnp.sqrt(precision_u)[:, None]).astype(jnp.bfloat16)
    col_share = lax.psum_scatter(jnp.sum(weight, axis=0), "row", scatter_dimension=0, tiled=True)

    def group_product(index):
        left = lax.dynamic_slice_in_dim(scaled, index * group, group, 1)
        product = lax.dot_general(
            left, scaled, (((0,), (0,)), ((), ())), preferred_element_type=jnp.float32
        )
        return product.astype(jnp.bfloat16)

    grouped = lax.map(group_product, jnp.arange(rows_n))
    arrived = lax.all_to_all(grouped, "row", split_axis=0, concat_axis=0, tiled=True)
    cross = jnp.sum(arrived, axis=0, dtype=jnp.float32)
    global_rows = row_idx * group + jnp.arange(group)
    diag_part = jnp.where(
        global_rows[:, None] == jnp.arange(width)[None, :], col_share[:, None], 0.0
    )
    strip = (diag_part - cross).reshape(per_row, tile, kcount, tile)
    residue = block_list % cols_n
    same = residue[:, :, None] == residue[:, None, :]
    before = jnp.arange(kcount)[None, :] < jnp.arange(kcount)[:, None]
    rank = jnp.sum((same & before[None]).astype(jnp.int32), axis=2)
    my_res = lax.dynamic_index_in_dim(residue, col_idx, 0, keepdims=False)
    my_rank = lax.dynamic_index_in_dim(rank, col_idx, 0, keepdims=False)
    chooser = (
        (my_res[None, None, :] == jnp.arange(cols_n)[:, None, None])
        & (my_rank[None, None, :] == jnp.arange(slots)[None, :, None])
    ).astype(jnp.float32)
    outgoing = jnp.einsum("csk,jakb->csjab", chooser, strip, precision=highest)
    incoming = lax.all_to_all(outgoing, "col", split_axis=0, concat_axis=0, tiled=True)
    picks = (residue == col_idx)[:, None, :] & (
        rank[:, None, :] == jnp.arange(slots)[None, :, None]
    )
    col_block = jnp.sum(jnp.where(picks, block_list[:, None, :], 0), axis=2)
    valid = jnp.any(picks, axis=2)
    row_block = lax.dynamic_slice_in_dim(block_list, row_idx * per_row, per_row, 1)
    local = row_block[:, None, :] // rows_n * nb_c + col_block[:, :, None] // cols_n
    local = jnp.where(valid[:, :, None], local, -1)
    placer = (jnp.arange(nb_r * nb_c)[:, None] == local.reshape(1, -1)).astype(jnp.float32)
    tiles = jnp.dot(placer, incoming.reshape(-1, tile * tile), precision=highest)
    row_ids = jnp.arange(nb_r) * rows_n + row_idx
    col_ids = jnp.arange(nb_c) * cols_n + col_idx
    on_diag = (row_ids[:, None] == col_ids[None, :])[:, :, None, None]
    schur = tiles.reshape(nb_r, nb_c, tile, tile) + jnp.where(
        on_diag, item_prior * jnp.eye(tile, dtype=jnp.float32)[None, None], 0.0
    )
    width_p = PANEL_BLOCKS * tile
    first_col = schur[:, 0]
    slot_mask = (jnp.arange(PANEL_BLOCKS) == col_idx).astype(jnp.float32)
    placed = first_col[:, :, None, :] * slot_mask[None, None, :, None]
    panel = lax.psum(placed, "col").reshape(nb_r, tile, width_p)
    row_mask = (jnp.arange(PANEL_BLOCKS) == row_idx).astype(jnp.float32)
    corner = lax.psum(panel[0][None] * row_mask[:, None, None], "row").reshape(width_p, width_p)
    lower = jnp.linalg.cholesky(corner)
    logdet = 2.0 * jnp.sum(jnp.log(jnp.diagonal(lower)))
    factor_rows = lax.linalg.triangular_solve(
        lower, panel.reshape(nb_r * tile, width_p), left_side=False, lower=True, transpose_a=True
    ).reshape(nb_r, tile, width_p)
    ratio = cols_n // rows_n
    strided = factor_rows.reshape(nb_c, ratio, tile, width_p)
    chosen = lax.dynamic_index_in_dim(strided, col_idx // rows_n, 1, keepdims=False)
    factor_cols = broadcast(chosen, "row", col_idx % rows_n)
    update = jnp.einsum("isk,jtk->ijst", factor_rows, factor_cols, precision=highest)
    own_panel = lax.dynamic_slice_in_dim(
        factor_rows, jnp.minimum(col_idx, PANEL_BLOCKS - 1) * tile, tile, 2
    )
    in_panel = col_ids < PANEL_BLOCKS
    above = row_ids < PANEL_BLOCKS
    trailing = jnp.where(above[:, None, None, None], 0.0, schur - update)
    result = jnp.where(in_panel[None, :, None, None], own_panel[:, None], trailing)
    tile_diag = jnp.diagonal(result, axis1=2, axis2=3)
    diag_vals = jnp.sum(jnp.where(on_diag[:, :, :, 0], tile_diag, 0.0), axis=0)
    pivot_part = lax.psum_scatter(
        diag_vals.reshape(nb_c * tile), "row", scatter_dimension=0, tiled=True
    )
    pivots = pivot_part.reshape(1, 1, pivot_part.shape[0])
    diag_entry = on_diag & jnp.eye(tile, dtype=bool)[None, None]
    cleared = jnp.where(diag_entry, 0.0, result)
    factored = cleared.transpose(0, 2, 1, 3)[:, None, :, :, None, :]
    trailing_mask = (
        jnp.logical_not(above)[:, None, None, None] & jnp.logical_not(in_panel)[None, :, None, None]
    )
    rounded_update = jnp.where(trailing_mask, update, 0.0).astype(jnp.bfloat16)
    corrected = rounded_update.transpose(0, 2, 1, 3)[:, None, :, :, None, :]
    return (factored, corrected, logdet, pivots)


def solution(mesh):
    in_specs = (P("col", "row", None), P("col", "row"), P(), P())
    out_specs = (
        P(None, "row", None, None, "col", None),
        P(None, "row", None, None, "col", None),
        P(),
        P("row", "col", None),
    )
    return jax.shard_map(body, mesh=mesh, in_specs=in_specs, out_specs=out_specs, check_vma=False)
```

profile of v0, /device:TPU:1, one launch (start us, length us, event | category | flops | bytes accessed | tf_op | source)
XLA Modules:
  0.0 953.2 jit_solution(7853409648612952227)
XLA Ops:
  9.0 2.2 fusion.43
  11.4 38.4 %while.11 = (s32[]{:T(128)}, bf16[16,128,2048]{2,1,0:T(8,128)(2,1)}, s32[16]{0:T(128)S(1)}, bf16[192,2048]{1,0:T(8,128)(2,1)S(1)}, s32[]{:T(128)}, /*index=5*/s32[1]{0:T(128)}, s32[]{:T(128)}, s32[]{:T(128)}) while((s32[]{:T(128)}, bf16[16,128,2048]{2,1,0:T(8,128)(2,1)}, s32[16]{0:T(128)S(1)}, bf16[192,2048]{1,0:T(8,128)(2,1)S(1)}, s32[]{:T(128)}, ...), condition=%wide.region_7.8_spmd, body=%wide.region_6.7_spmd.sunk | while | flops 100925448 | bytes 1360031 | solution.py:49
  49.8 7.6 all-to-all-start
  59.4 131.3 %all-reduce.1 = f32[2048]{0:T(1024)S(1)} all-reduce(f32[2048]{0:T(1024)S(1)} %get-tuple-element.51), channel_id=2, replica_groups=mesh['row'=16,'col'=32] {'row'}, use_global_device_ids=true, to_apply=%region_4.5.clone | all-reduce | flops 2048 | bytes 16384
  191.1 5.3 convert_reduce_fusion
  197.9 2.5 copy.49
  200.5 60.7 %all-to-all-start.1 = ((f32[32,1,1,128,128]{4,3,2,1,0:T(8,128)}), f32[32,1,1,128,128]{4,3,2,1,0:T(8,128)}, u32[]{:S(2)}, u32[]{:S(2)}) async-start(f32[32,1,1,128,128]{4,3,2,1,0:T(8,128)} %copy.49), calls=%async_computation.1 | async-start | bytes 4194304 | tf_op jit(solution)/shard_map/all_to_all | solution.py:68
  261.5 98.1 %all-to-all-done.1 = f32[32,1,1,128,128]{4,3,2,1,0:T(8,128)} async-done(((f32[32,1,1,128,128]{4,3,2,1,0:T(8,128)}), f32[32,1,1,128,128]{4,3,2,1,0:T(8,128)}, u32[]{:S(2)}, u32[]{:S(2)}) %all-to-all-start.1) | async-done | bytes 2097184 | tf_op jit(solution)/shard_map/all_to_all | solution.py:68
  359.6 5.3 select_add_fusion
  366.4 204.2 %all-reduce.7.cloned.1.call-done = f32[8,128,2,128]{1,0,3,2:T(8,128)} async-done(((f32[8,128,2,128]{1,0,3,2:T(8,128)}), f32[8,128,2,128]{1,0,3,2:T(8,128)}) %all-reduce.7.cloned.1.call-update) | async-done | bytes 1048592 | tf_op jit(solution)/shard_map/psum | solution.py:89
  575.4 111.9 %all-reduce.9.cloned.1.call-done = f32[256,256]{0,1:T(8,128)} async-done(((f32[256,256]{0,1:T(8,128)}), f32[256,256]{0,1:T(8,128)}) %all-reduce.9.cloned.1.call-update) | async-done | bytes 262160 | tf_op jit(solution)/shard_map/psum | solution.py:91
  689.4 11.7 %cholesky.40 = f32[128,128]{1,0:T(8,128)S(1)} custom-call(f32[128,128]{1,0:T(8,128)S(1)} %cholesky.100), custom_call_target="Cholesky" | custom-call | tf_op jit(solution)/shard_map/jit(cholesky)/cholesky | solution.py:92
  701.1 9.8 %custom-call.14 = f32[1,128,128]{1,2,0:T(8,128)S(1)} custom-call(f32[1,128,128]{2,1,0:T(8,128)S(1)} %get-tuple-element.81), custom_call_target="InvertDiagBlocksLowerTriangular" | custom-call | tf_op jit(solution)/shard_map/jit(cholesky)/cholesky | solution.py:92
  711.4 11.7 %cholesky.87 = f32[128,128]{1,0:T(8,128)S(1)} custom-call(f32[128,128]{1,0:T(8,128)S(1)} %convolution_subtract_fusion.1), custom_call_target="Cholesky" | custom-call | tf_op jit(solution)/shard_map/jit(cholesky)/cholesky | solution.py:92
  726.0 5.8 while.12
  727.1 2.0 bitcast_dynamic-update-slice_fusion.2
  729.7 2.0 bitcast_dynamic-update-slice_fusion.2
  732.5 21.1 %custom-call.15 = f32[2,128,128]{1,2,0:T(8,128)} custom-call(f32[2,128,128]{2,1,0:T(8,128)} %get-tuple-element.34), custom_call_target="InvertDiagBlocksLowerTriangular" | custom-call | tf_op jit(solution)/shard_map/triangular_solve | solution.py:94
  753.6 1.7 fusion.15
  755.3 1.8 convolution_subtract_fusion
  757.7 1.6 pad_maximum_fusion
  759.3 2.1 reshape_reshape.7
  767.2 2.1 copy.70
  769.2 1.5 copy.65
  770.7 2.5 gather_fusion
  774.5 106.3 %all-reduce.11.cloned.1.call-done = f32[4,128,256]{2,1,0:T(8,128)} async-done(((f32[4,128,256]{2,1,0:T(8,128)}), f32[4,128,256]{2,1,0:T(8,128)}) %all-reduce.11.cloned.1.call-update) | async-done | bytes 524304 | tf_op jit(solution)/shard_map/psum | solution.py:16
  880.8 4.7 fusion.7
  886.1 3.5 copy.61
  889.9 1.8 copy.62
  891.7 19.8 %copy.59 = f32[8,4,128,128]{0,1,3,2:T(4,128)} copy(f32[8,4,128,128]{3,0,2,1:T(8,128)S(1)} %copy-done.2) | data formatting | bytes 4194304 | tf_op jit(solution)/shard_map/jit(_where)/select_n | solution.py:108
  911.5 1.9 gather_fusion.1
  913.7 31.1 %all-reduce.2 = f32[512]{0:T(512)S(1)} all-reduce(f32[512]{0:T(512)S(1)} %bitcast.178), channel_id=3, replica_groups=mesh['row'=16,'col'=32] {'row'}, use_global_device_ids=true, to_apply=%region_18.19.clone | all-reduce | flops 512 | bytes 4096
  (133 shorter events, 53.4 us)
Async XLA Ops:
  7.2 1.7 copy-start
  49.8 141.3 %all-to-all-start = ((bf16[16,128,2048]{2,1,0:T(8,128)(2,1)}), bf16[16,128,2048]{2,1,0:T(8,128)(2,1)}, u32[]{:S(2)}, u32[]{:S(2)}) async-start(bf16[16,128,2048]{2,1,0:T(8,128)(2,1)} %get-tuple-element.26), calls=%async_computation | async-start | bytes 16777216 | tf_op jit(solution)/shard_map/all_to_all | solution.py:50
  200.5 60.8 %copy-start.10 = (s32[32,16]{0,1:T(8,128)S(1)}, s32[32,16]{0,1:T(8,128)}, u32[]{:S(2)}) copy-start(s32[32,16]{0,1:T(8,128)} %param.9) | copy-start | bytes 6148
  200.5 159.1 %all-to-all-start.1 = ((f32[32,1,1,128,128]{4,3,2,1,0:T(8,128)}), f32[32,1,1,128,128]{4,3,2,1,0:T(8,128)}, u32[]{:S(2)}, u32[]{:S(2)}) async-start(f32[32,1,1,128,128]{4,3,2,1,0:T(8,128)} %copy.49), calls=%async_computation.1 | async-start | bytes 4194304 | tf_op jit(solution)/shard_map/all_to_all | solution.py:68
  261.2 309.4 %all-reduce.7.cloned.1.call-start = ((), (), s32[]{:S(2)}) async-start(), calls=%async_computation.2 | async-start | bytes 2097152 | tf_op jit(solution)/shard_map/psum | solution.py:89
  366.4 320.9 %all-reduce.9.cloned.1.call-start = ((), (), s32[]{:S(2)}) async-start(), calls=%async_computation.3 | async-start | bytes 524288 | tf_op jit(solution)/shard_map/psum | solution.py:91
  570.6 3.3 copy-start.8
  572.9 307.8 %all-reduce.11.cloned.1.call-start = ((), (), s32[]{:S(2)}) async-start(), calls=%async_computation.4 | async-start | bytes 1048576 | tf_op jit(solution)/shard_map/psum | solution.py:16
  574.2 1.0 copy-start.6
  731.8 0.7 copy-start.7
  753.6 3.5 copy-start.9
  770.7 110.0 %copy-start.5 = (f32[8,128,256,1]{2,0,1,3:T(8,128)S(1)}, f32[8,128,256,1]{2,0,1,3:T(8,128)}, u32[]{:S(2)}) copy-start(f32[8,128,256,1]{2,0,1,3:T(8,128)} %copy.65) | copy-start | bytes 3145732
  880.8 4.7 copy-start.3
  880.8 4.7 copy-start.4
  889.6 2.0 copy-start.2
  891.7 53.7 %copy-start.1 = (f32[128,128]{1,0:T(8,128)S(1)}, f32[128,128]{1,0:T(8,128)}, u32[]{:S(2)}) copy-start(f32[128,128]{1,0:T(8,128)} %param.8) | copy-start | bytes 196612
Sparse Core Ops, SparseCore 0:
  366.5 204.1 all-reduce.6
  573.8 113.4 all-reduce.8
  765.0 115.7 all-reduce.10
where the time goes:
time: 970 us; the launch traced here: 953 us
  waiting for transfers between devices  520 us (54%)
  blocking collectives  162 us (17%)
  other arithmetic  71.6 us (7%)
  starting transfers between devices  68.8 us (7%)
  local copies, waits for them, and re-layouts  65.8 us (7%)
  matrix products  34.4 us (4%)
  between operations  18.8 us (2%)
  loops' own time  11 us (1%)
    psum x1, waiting for transfers between devices, body(): panel = lax.psum(placed, 'col').reshape(nb_r, tile, width_p)  204 us
    unnamed x2, blocking collectives  162 us
    psum x1, waiting for transfers between devices, body(): lax.psum(panel[0][None] * row_mask[:, None, None], 'row')  112 us
    psum x1, waiting for transfers between devices, broadcast(): return lax.psum(block, axis)  106 us
    all_to_all x1, waiting for transfers between devices, body(): lax.all_to_all(outgoing, 'col', split_axis=0, concat_axis=0, tiled=True)  98.1 us
    all_to_all x1, starting transfers between devices, body(): lax.all_to_all(outgoing, 'col', split_axis=0, concat_axis=0, tiled=True)  60.7 us
    another operation x7, other arithmetic, body(): lower = jnp.linalg.cholesky(corner)  34.7 us
    another operation x4, other arithmetic, body(): lax.linalg.triangular_solve(lower, panel.reshape(nb_r * tile, width_p), l...  22.7 us
  transfers between devices with their start and end apart: 5, of which 4 were waited for; matrix products, arithmetic and copies ran while one was open for 1% of the time, Pallas kernels for 0%

commit v1 on v0

v1 whole, which is shorter than its diff:
```python
import jax
import jax.numpy as jnp
from jax import lax
from jax.sharding import PartitionSpec as P

PANEL_BLOCKS = 2


highest = lax.Precision.HIGHEST
user_prior = 1.0
item_prior = 1.0


def body(observed, user_effect, item_effect, block_list):
    rows_n = lax.axis_size("row")
    cols_n = lax.axis_size("col")
    row_idx = lax.axis_index("row")
    col_idx = lax.axis_index("col")
    nblocks, tile = item_effect.shape
    kcount = block_list.shape[1]
    per_row = kcount // rows_n
    slots = max(1, kcount // cols_n)
    width = kcount * tile
    group = per_row * tile
    nb_r = nblocks // rows_n
    nb_c = nblocks // cols_n
    width_p = PANEL_BLOCKS * tile
    mine = lax.dynamic_index_in_dim(block_list, col_idx, 0, keepdims=False)
    picker = (mine[:, None] == jnp.arange(nblocks)[None, :]).astype(jnp.float32)
    item_vals = jnp.dot(picker, item_effect, precision=highest).reshape(width)
    marks = observed[0]
    prob = jax.nn.sigmoid(user_effect[0][:, None] + item_vals[None, :])
    weight = jnp.where(marks > 0, prob * (1.0 - prob), 0.0)
    precision_u = user_prior + jnp.sum(weight, axis=1)
    scaled = (weight / jnp.sqrt(precision_u)[:, None]).astype(jnp.bfloat16)
    col_share = lax.psum_scatter(jnp.sum(weight, axis=0), "row", scatter_dimension=0, tiled=True)

    product = lax.dot_general(
        scaled, scaled, (((0,), (0,)), ((), ())), preferred_element_type=jnp.float32
    ).astype(jnp.bfloat16)
    grouped = product.reshape(rows_n, group, width)
    arrived = lax.all_to_all(grouped, "row", split_axis=0, concat_axis=0, tiled=True)
    cross = jnp.sum(arrived, axis=0, dtype=jnp.float32)
    global_rows = row_idx * group + jnp.arange(group)
    diag_part = jnp.where(
        global_rows[:, None] == jnp.arange(width)[None, :], col_share[:, None], 0.0
    )
    strip = (diag_part - cross).reshape(per_row, tile, kcount, tile)
    row_block = lax.dynamic_slice_in_dim(mine, row_idx * per_row, per_row, 0)

    holds = mine[None, :] == jnp.arange(PANEL_BLOCKS)[:, None]
    panel_part = jnp.sum(
        jnp.where(holds[None, None, :, :, None], strip[:, :, None, :, :], 0.0), axis=3
    )
    at_row = (row_block[:, None] // rows_n) == jnp.arange(nb_r)[None, :]
    placed = jnp.sum(
        jnp.where(at_row[:, :, None, None, None], panel_part[:, None], 0.0), axis=0
    )
    row_ids = jnp.arange(nb_r) * rows_n + row_idx
    col_ids = jnp.arange(nb_c) * cols_n + col_idx
    eye = jnp.eye(tile, dtype=jnp.float32)
    panel_eye = jnp.where(
        (row_ids[:, None] == jnp.arange(PANEL_BLOCKS)[None, :])[:, None, :, None],
        item_prior * eye[None, :, None, :],
        0.0,
    )
    panel = lax.psum(placed, "col") + panel_eye

    residue = block_list % cols_n
    same = residue[:, :, None] == residue[:, None, :]
    before = jnp.arange(kcount)[None, :] < jnp.arange(kcount)[:, None]
    rank = jnp.sum((same & before[None]).astype(jnp.int32), axis=2)
    my_res = lax.dynamic_index_in_dim(residue, col_idx, 0, keepdims=False)
    my_rank = lax.dynamic_index_in_dim(rank, col_idx, 0, keepdims=False)
    chooser = (
        (my_res[None, None, :] == jnp.arange(cols_n)[:, None, None])
        & (my_rank[None, None, :] == jnp.arange(slots)[None, :, None])
    ).astype(jnp.float32)
    outgoing = jnp.einsum("csk,jakb->csjab", chooser, strip, precision=highest)
    incoming = lax.all_to_all(outgoing, "col", split_axis=0, concat_axis=0, tiled=True)
    picks = (residue == col_idx)[:, None, :] & (
        rank[:, None, :] == jnp.arange(slots)[None, :, None]
    )
    col_block = jnp.sum(jnp.where(picks, block_list[:, None, :], 0), axis=2)
    valid = jnp.any(picks, axis=2)
    row_blocks = lax.dynamic_slice_in_dim(block_list, row_idx * per_row, per_row, 1)
    sel = (
        valid[:, :, None, None, None]
        & ((row_blocks[:, None, :] // rows_n)[:, :, :, None, None] == jnp.arange(nb_r)[None, None, None, :, None])
        & ((col_block[:, :, None] // cols_n)[:, :, :, None, None] == jnp.arange(nb_c)[None, None, None, None, :])
    )
    on_diag = row_ids[:, None] == col_ids[None, :]
    tiles = jnp.einsum(
        "cvjiq,cvjst->isqt",
        sel.astype(jnp.float32),
        incoming,
        precision=highest,
    )
    schur = tiles + jnp.where(on_diag[:, None, :, None], item_prior * eye[None, :, None, :], 0.0)

    top = (row_idx < PANEL_BLOCKS).astype(jnp.float32)
    first = (jnp.arange(PANEL_BLOCKS) == row_idx).astype(jnp.float32)
    col_panel = schur[0].transpose(1, 0, 2)[:, None] * first[None, :, None, None]
    corner_part = panel[0][None] * first[:, None, None, None] * top
    diag_tile = jnp.diagonal(schur, axis1=1, axis2=3)
    diag_vals = jnp.sum(jnp.where(on_diag[:, :, None], diag_tile, 0.0), axis=0)
    sizes = (col_panel.size, corner_part.size, diag_vals.size)
    packed = jnp.concatenate(
        [col_panel.reshape(-1), corner_part.reshape(-1), diag_vals.reshape(-1)]
    )
    shared = lax.psum(packed, "row")
    col_panel = shared[: sizes[0]].reshape(nb_c, PANEL_BLOCKS, tile, tile)
    corner = shared[sizes[0] : sizes[0] + sizes[1]].reshape(width_p, width_p)
    col_diag = shared[sizes[0] + sizes[1] :].reshape(nb_c, tile)

    lower = jnp.linalg.cholesky(corner)
    logdet = 2.0 * jnp.sum(jnp.log(jnp.diagonal(lower)))
    panel_cols = col_panel.transpose(0, 3, 1, 2).reshape(nb_c * tile, width_p)
    rhs = jnp.concatenate([panel.reshape(nb_r * tile, width_p), panel_cols], axis=0)
    solved = lax.linalg.triangular_solve(
        lower, rhs, left_side=False, lower=True, transpose_a=True
    )
    factor_rows = solved[: nb_r * tile].reshape(nb_r, tile, width_p)
    factor_cols = solved[nb_r * tile :].reshape(nb_c, tile, width_p)
    update = jnp.einsum("isk,jtk->isjt", factor_rows, factor_cols, precision=highest)
    own_panel = lax.dynamic_slice_in_dim(
        factor_rows, jnp.minimum(col_idx, PANEL_BLOCKS - 1) * tile, tile, 2
    )
    in_panel = col_ids < PANEL_BLOCKS
    above = row_ids < PANEL_BLOCKS
    trailing = jnp.where(above[:, None, None, None], 0.0, schur - update)
    result = jnp.where(in_panel[None, None, :, None], own_panel[:, :, None, :], trailing)
    diag_entry = on_diag[:, None, :, None] & eye.astype(bool)[None, :, None, :]
    cleared = jnp.where(diag_entry, 0.0, result)
    factored = cleared[:, None, :, :, None, :]
    trailing_mask = (
        jnp.logical_not(above)[:, None, None, None] & jnp.logical_not(in_panel)[None, None, :, None]
    )
    rounded_update = jnp.where(trailing_mask, update, 0.0).astype(jnp.bfloat16)
    corrected = rounded_update[:, None, :, :, None, :]

    share = nblocks * tile // (rows_n * cols_n)
    start = row_idx * share
    piv_jj = start // tile
    piv_s = start % tile
    piv_block = piv_jj * cols_n + col_idx
    piv_rows = lax.dynamic_slice_in_dim(
        lax.dynamic_index_in_dim(factor_cols, piv_jj, 0, keepdims=False), piv_s, share, 0
    )
    piv_diag = lax.dynamic_slice_in_dim(
        lax.dynamic_index_in_dim(col_diag, piv_jj, 0, keepdims=False), piv_s, share, 0
    )
    trail_piv = piv_diag - jnp.sum(piv_rows * piv_rows, axis=1)
    panel_at = piv_block * tile + piv_s + jnp.arange(share)
    panel_piv = jnp.sum(
        jnp.where(panel_at[:, None] == jnp.arange(width_p)[None, :], piv_rows, 0.0), axis=1
    )
    piv = jnp.where(piv_block < PANEL_BLOCKS, panel_piv, trail_piv)
    pivots = piv.reshape(1, 1, share)
    return (factored, corrected, logdet, pivots)


def solution(mesh):
    in_specs = (P("col", "row", None), P("col", "row"), P(), P())
    out_specs = (
        P(None, "row", None, None, "col", None),
        P(None, "row", None, None, "col", None),
        P(),
        P("row", "col", None),
    )
    return jax.shard_map(body, mesh=mesh, in_specs=in_specs, out_specs=out_specs, check_vma=False)
```

time: 970 us -> 736 us (0.76)
  waiting for transfers between devices: 520 us -> 337 us
  blocking collectives: 162 us -> 131 us
  matrix products: 34.4 us -> 22.2 us
  starting transfers between devices: 68.8 us -> 80.1 us
  loops' own time: 11 us -> 0.01 us
  local copies, waits for them, and re-layouts: 65.8 us -> 55.3 us
    all_to_all x1, waiting for transfers between devices: 98.1 us -> 0.01 us  [body(): lax.all_to_all(outgoing, 'col', split_axis=0, concat_axis=0, tiled=True)]
    psum x3 -> x2, waiting for transfers between devices: 422 us -> 337 us  [the longest x1 223 us: body(): panel = lax.psum(placed, 'col') + panel_eye]
    unnamed x2 -> x1, blocking collectives: 162 us -> 131 us
    add x0 -> x1, local copies, waits for them, and re-layouts: none -> 22.5 us  [body(): tiles + jnp.where(on_diag[:, None, :, None], item_prior * eye[None, :, No...]
    select_n x1 -> x0, local copies, waits for them, and re-layouts: 19.8 us -> none  [body(): jnp.where(in_panel[None, :, None, None], own_panel[:, None], trailing)]
    dot_general x18 -> x3, matrix products: 28.5 us -> 13.5 us  [the longest x1 6.32 us: body(): lax.dot_general(scaled, scaled, (((0,), (0,)), ((), ())), preferred_eleme...]
    another operation x2 -> x1, loops' own time: 11 us -> 0.01 us  [body(): lax.linalg.triangular_solve(lower, rhs, left_side=False, lower=True, tran...]
    psum x3 -> x2, starting transfers between devices: 0.38 us -> 10.9 us  [the longest x1 10.8 us: body(): shared = lax.psum(packed, 'row')]
  transfers between devices with their start and end apart: 5 -> 4, of which waited for: 4 -> 2; matrix products, arithmetic and copies ran while one was open for 1% -> 1% of each run, Pallas kernels for 0% -> 0%
where the time goes in v1:
time: 736 us; the launch traced here: 726 us
  waiting for transfers between devices  337 us (46%)
  blocking collectives  131 us (18%)
  starting transfers between devices  80.1 us (11%)
  other arithmetic  78.8 us (11%)
  local copies, waits for them, and re-layouts  55.3 us (8%)
  matrix products  22.2 us (3%)
  between operations  21.4 us (3%)
    psum x1, waiting for transfers between devices, body(): panel = lax.psum(placed, 'col') + panel_eye  223 us
    unnamed x1, blocking collectives  131 us
    psum x1, waiting for transfers between devices, body(): shared = lax.psum(packed, 'row')  114 us
    all_to_all x1, starting transfers between devices, body(): lax.all_to_all(outgoing, 'col', split_axis=0, concat_axis=0, tiled=True)  61.6 us
    another operation x7, other arithmetic, body(): lower = jnp.linalg.cholesky(corner)  34.6 us
    add x1, local copies, waits for them, and re-layouts, body(): tiles + jnp.where(on_diag[:, None, :, None], item_prior * eye[None, :, No...  22.5 us
    another operation x4, other arithmetic, body(): lax.linalg.triangular_solve(lower, rhs, left_side=False, lower=True, tran...  21.7 us
  transfers between devices with their start and end apart: 4, of which 2 were waited for; matrix products, arithmetic and copies ran while one was open for 1% of the time, Pallas kernels for 0%

profile of v1, /device:TPU:1, one launch (start us, length us, event | category | flops | bytes accessed | tf_op | source)
XLA Modules:
  0.0 725.8 jit_solution(9679253529761902558)
XLA Ops:
  9.0 2.4 fusion.24
  11.4 6.3 convolution_convert_fusion
  17.7 7.6 %all-to-all-start = ((bf16[16,128,2048]{2,1,0:T(8,128)(2,1)}), bf16[16,128,2048]{2,1,0:T(8,128)(2,1)}, u32[]{:S(2)}, u32[]{:S(2)}) async-start(bf16[16,128,2048]{2,1,0:T(8,128)(2,1)} %bitcast.138), calls=%async_computation | async-start | bytes 16777216 | tf_op jit(solution)/shard_map/all_to_all | solution.py:42
  27.3 130.5 %all-reduce.1 = f32[2048]{0:T(1024)S(1)} all-reduce(f32[2048]{0:T(1024)S(1)} %get-tuple-element.32), channel_id=2, replica_groups=mesh['row'=16,'col'=32] {'row'}, use_global_device_ids=true, to_apply=%region_1.2.clone | all-reduce | flops 2048 | bytes 16384
  158.2 5.3 convert_reduce_fusion
  165.0 2.5 copy.60
  167.6 61.6 %all-to-all-start.1 = ((f32[32,1,1,128,128]{4,3,2,1,0:T(8,128)}), f32[32,1,1,128,128]{4,3,2,1,0:T(8,128)}, u32[]{:S(2)}, u32[]{:S(2)}) async-start(f32[32,1,1,128,128]{4,3,2,1,0:T(8,128)} %copy.60), calls=%async_computation.1 | async-start | bytes 4194304 | tf_op jit(solution)/shard_map/all_to_all | solution.py:80
  235.5 1.4 broadcast_select_fusion
  236.9 10.8 %all-reduce.7.cloned.1.call-start = ((), (), s32[]{:S(2)}) async-start(), calls=%async_computation.3 | async-start | bytes 1581056 | tf_op jit(solution)/shard_map/psum | solution.py:111
  248.3 223.2 %all-reduce.5.cloned.1.call-done = f32[8,128,2,128]{3,2,1,0:T(2,128)} async-done(((f32[8,128,2,128]{3,2,1,0:T(2,128)}), f32[8,128,2,128]{3,2,1,0:T(2,128)}) %all-reduce.5.cloned.1.call-update) | async-done | bytes 1048592 | tf_op jit(solution)/shard_map/psum | solution.py:67
  471.5 1.8 select_add_fusion
  473.5 4.0 bitcast_add_fusion.1
  477.5 1.7 bitcast_add_fusion
  479.2 22.5 %copy.63 = f32[8,4,128,128]{0,1,3,2:T(4,128)} copy(f32[8,4,128,128]{3,0,1,2:T(8,128)} %bitcast_add_fusion) | data formatting | bytes 4194304 | tf_op jit(solution)/shard_map/add | solution.py:99
  501.7 2.6 gather_fusion
  508.0 114.2 %all-reduce.7.cloned.1.call-done = f32[197120]{0:T(1024)} async-done(((f32[197120]{0:T(1024)}), f32[197120]{0:T(1024)}) %all-reduce.7.cloned.1.call-update) | async-done | bytes 788496 | tf_op jit(solution)/shard_map/psum | solution.py:111
  623.5 11.7 %cholesky.39 = f32[128,128]{1,0:T(8,128)S(1)} custom-call(f32[128,128]{1,0:T(8,128)S(1)} %cholesky.97), custom_call_target="Cholesky" | custom-call | tf_op jit(solution)/shard_map/jit(cholesky)/cholesky | solution.py:116
  635.2 9.8 %custom-call.14 = f32[1,128,128]{1,2,0:T(8,128)S(1)} custom-call(f32[1,128,128]{2,1,0:T(8,128)S(1)} %get-tuple-element.54), custom_call_target="InvertDiagBlocksLowerTriangular" | custom-call | tf_op jit(solution)/shard_map/jit(cholesky)/cholesky | solution.py:116
  647.2 11.7 %cholesky.84 = f32[128,128]{1,0:T(8,128)S(1)} custom-call(f32[128,128]{1,0:T(8,128)S(1)} %convolution_subtract_fusion.1), custom_call_target="Cholesky" | custom-call | tf_op jit(solution)/shard_map/jit(cholesky)/cholesky | solution.py:116
  661.7 5.2 while.1
  662.3 2.0 bitcast_dynamic-update-slice_fusion.4
  664.9 2.0 bitcast_dynamic-update-slice_fusion.4
  666.9 21.2 %custom-call.15 = f32[2,128,128]{1,2,0:T(8,128)} custom-call(f32[2,128,128]{2,1,0:T(8,128)} %get-tuple-element.11), custom_call_target="InvertDiagBlocksLowerTriangular" | custom-call | tf_op jit(solution)/shard_map/triangular_solve | solution.py:120
  689.1 2.1 fusion.12
  691.2 2.2 convolution_subtract_fusion
  697.5 1.4 copy.84
  698.9 1.5 copy.75
  702.5 3.2 fusion.19
  706.6 3.5 copy.72
  710.4 1.4 copy.73
  711.8 2.3 gather_fusion.1
  714.8 1.4 constant_dynamic-slice_fusion.1
  (120 shorter events, 28.5 us)
Async XLA Ops:
  7.2 1.7 copy-start
  7.2 4.2 copy-start.9
  17.7 140.5 %all-to-all-start = ((bf16[16,128,2048]{2,1,0:T(8,128)(2,1)}), bf16[16,128,2048]{2,1,0:T(8,128)(2,1)}, u32[]{:S(2)}, u32[]{:S(2)}) async-start(bf16[16,128,2048]{2,1,0:T(8,128)(2,1)} %bitcast.138), calls=%async_computation | async-start | bytes 16777216 | tf_op jit(solution)/shard_map/all_to_all | solution.py:42
  167.6 61.7 %copy-start.7 = (s32[32,16]{0,1:T(8,128)S(1)}, s32[32,16]{0,1:T(8,128)}, u32[]{:S(2)}) copy-start(s32[32,16]{0,1:T(8,128)} %param.7) | copy-start | bytes 6148
  167.6 305.9 %all-to-all-start.1 = ((f32[32,1,1,128,128]{4,3,2,1,0:T(8,128)}), f32[32,1,1,128,128]{4,3,2,1,0:T(8,128)}, u32[]{:S(2)}, u32[]{:S(2)}) async-start(f32[32,1,1,128,128]{4,3,2,1,0:T(8,128)} %copy.60), calls=%async_computation.1 | async-start | bytes 4194304 | tf_op jit(solution)/shard_map/all_to_all | solution.py:80
  229.2 242.3 %all-reduce.5.cloned.1.call-start = ((), (), s32[]{:S(2)}) async-start(), calls=%async_computation.2 | async-start | bytes 2097152 | tf_op jit(solution)/shard_map/psum | solution.py:67
  236.9 385.3 %all-reduce.7.cloned.1.call-start = ((), (), s32[]{:S(2)}) async-start(), calls=%async_computation.3 | async-start | bytes 1581056 | tf_op jit(solution)/shard_map/psum | solution.py:111
  505.5 1.4 copy-start.12
  505.5 1.4 copy-start.13
  508.0 153.6 %copy-start.11 = (s32[2]{0:T(128)S(1)}, s32[2]{0:T(128)}, u32[]{:S(2)}) copy-start(s32[2]{0:T(128)} %iota_multiply_fusion) | copy-start | bytes 28
  623.4 11.8 %copy-start.6 = (f32[256,256]{1,0:T(8,128)}, f32[256,256]{1,0:T(8,128)S(1)}, u32[]{:S(2)}) copy-start(f32[256,256]{1,0:T(8,128)S(1)} %fusion.21) | copy-start | bytes 786436
  623.4 64.6 %slice-start = ((f32[197120]{0:T(1024)}), f32[131072]{0:T(1024)S(1)}, s32[]{:S(2)}) async-start(f32[197120]{0:T(1024)} %all-reduce.7.cloned.1.call-done), calls=%async_computation.4 | async-start | bytes 1048576 | tf_op jit(solution)/shard_map/slice | solution.py:112
  666.9 21.2 %copy-start.5 = (f32[256,256]{1,0:T(8,128)}, f32[256,256]{1,0:T(8,128)S(1)}, u32[]{:S(2)}) copy-start(f32[256,256]{1,0:T(8,128)S(1)} %get-tuple-element.116) | copy-start | bytes 786436
  689.1 2.1 copy-start.2
  689.1 4.4 copy-start.8
  695.7 0.8 copy-start.3
  702.5 3.2 copy-start.10
  710.1 7.4 %copy-start.1 = (f32[128,128]{1,0:T(8,128)S(1)}, f32[128,128]{1,0:T(8,128)}, u32[]{:S(2)}) copy-start(f32[128,128]{1,0:T(8,128)} %param.6) | copy-start | bytes 196612
  710.4 6.4 copy-start.4
Sparse Core Ops, SparseCore 0:
  237.0 234.4 all-reduce.4
  506.9 115.2 all-reduce.6
